TPU v7x, 512 devices: a whole 4x4x16 slice. The times are simulated.
512 devices in a mesh: tm: 32 (over z, x_hi), fsdp: 16 (over y, x_lo, core).
Axes of the slice: x: 4 (x_hi: 2, x_lo: 2; x = x_hi * 2 + x_lo), y: 4, z: 16, core: 2. Of those that a mesh axis runs over, the one named last changes fastest.
Arguments:
- latents: bfloat16 [32768, 3072], P(('tm', 'fsdp')), may hold values from -6 to 6
- projected: bfloat16 [32768, 3, 2048], P(('tm', 'fsdp')), may hold values from -20 to 20
- out_weight: bfloat16 [2048, 3072], P(None, 'fsdp'), may hold values from -0.5 to 0.5
- gate_table: float32 [40, 3072], replicated, may hold values from 0.25 to 2
- timesteps: int32 [128], P('tm'), may hold values from 0 to 39
Outputs:
- updated: bfloat16 [32768, 3072], P(('tm', 'fsdp'))
All inputs are finite; a program needn't handle non-finite values.
Results may differ from a plain program's by a relative error of at most 0.0085.
Values may be sent and summed in bfloat16 or wider, within the bound.
No kernel may reach another device: no remote copies, remote signals or barrier semaphores. Data moves between devices by JAX's collectives and lax.ppermute only.
A program may use at most 64 MiB of HBM per device.

v0:
```python
import jax
import jax.numpy as jnp
from jax import lax
from jax.sharding import PartitionSpec as P

FRAME_TOK = 256


def passed_along(value, axis, steps):
    count = lax.axis_size(axis)
    initial, last = (max(0, -steps), min(count, count - steps))
    return lax.ppermute(value, axis, [(source, source + steps) for source in range(initial, last)])


def attend(queries, extended, first_frame, frame_count):
    pair_rows = 2 * FRAME_TOK
    key_count = 5 * FRAME_TOK
    score_scale = queries.shape[1] ** (-0.5)
    row_frame = jnp.arange(pair_rows, dtype=jnp.int32) // FRAME_TOK
    col_frame = jnp.arange(key_count, dtype=jnp.int32) // FRAME_TOK

    def frame_pair(pair_index):
        offset = pair_index * pair_rows
        query_block = lax.dynamic_slice_in_dim(queries, offset, pair_rows, 0)
        window = lax.dynamic_slice_in_dim(extended, offset, key_count, 0)
        key_block = window[:, 0]
        value_block = window[:, 1]
        scores = (
            lax.dot_general(
                query_block, key_block, (((1,), (1,)), ((), ())), preferred_element_type=jnp.float32
            )
            * score_scale
        )
        distance = col_frame[None, :] - row_frame[:, None]
        existing = first_frame + 2 * pair_index + col_frame - 3 >= 0
        allowed = (distance >= 0) & (distance <= 3) & existing[None, :]
        scores = jnp.where(allowed, scores, -1e30)
        row_max = jnp.max(scores, axis=-1, keepdims=True)
        weights = jnp.exp(scores - row_max)
        row_sum = jnp.sum(weights, axis=-1, keepdims=True)
        probability = (weights / row_sum).astype(jnp.bfloat16)
        return jnp.dot(probability, value_block, preferred_element_type=jnp.float32).astype(
            jnp.bfloat16
        )

    blocks = lax.map(frame_pair, jnp.arange(frame_count // 2, dtype=jnp.int32))
    return blocks.reshape(frame_count * FRAME_TOK, queries.shape[1])


def body(latents, projected, out_weight, gate_table, timesteps):
    row_count = latents.shape[0]
    frame_count = timesteps.shape[0]
    group_tokens = frame_count * FRAME_TOK
    head_view = lax.all_to_all(projected, "fsdp", split_axis=2, concat_axis=0, tiled=True)
    queries = head_view[:, 0]
    key_values = head_view[:, 1:3]
    trailing = passed_along(key_values[group_tokens - 3 * FRAME_TOK :], "tm", 1)
    extended = jnp.concatenate([trailing, key_values], axis=0)
    first_frame = lax.axis_index("tm") * frame_count
    attended = attend(queries, extended, first_frame, frame_count)
    gathered_heads = lax.all_to_all(attended, "fsdp", split_axis=0, concat_axis=1, tiled=True)
    update = jnp.dot(
        gathered_heads,
        lax.all_gather(out_weight, "fsdp", axis=1, tiled=True),
        preferred_element_type=jnp.float32,
    )
    step_count = gate_table.shape[0]
    step_onehot = (timesteps[:, None] == jnp.arange(step_count, dtype=jnp.int32)[None, :]).astype(
        jnp.float32
    )
    frame_gates = jnp.dot(step_onehot, gate_table, precision=lax.Precision.HIGHEST)
    row_frame = (
        lax.axis_index("fsdp") * row_count + jnp.arange(row_count, dtype=jnp.int32)
    ) // FRAME_TOK
    row_onehot = (row_frame[:, None] == jnp.arange(frame_count, dtype=jnp.int32)[None, :]).astype(
        jnp.float32
    )
    row_gates = jnp.dot(row_onehot, frame_gates, precision=lax.Precision.HIGHEST)
    return (latents.astype(jnp.float32) + row_gates * update).astype(jnp.bfloat16)


def solution(mesh):
    in_specs = (
        P(("tm", "fsdp"), None),
        P(("tm", "fsdp"), None, None),
        P(None, "fsdp"),
        P(),
        P("tm"),
    )
    out_specs = P(("tm", "fsdp"), None)
    return jax.shard_map(body, mesh=mesh, in_specs=in_specs, out_specs=out_specs, check_vma=False)
```

profile of v0, /device:TPU:1, one launch (start us, length us, event | category | flops | bytes accessed | tf_op | source)
XLA Modules:
  0.0 122.3 jit_solution(10871948725285879211)
XLA Ops:
  6.5 0.7 all-gather.2.cloned.1.call-update
  7.3 2.9 %copy.9 = bf16[64,3,2048]{0,1,2:T(4,128)(2,1)S(1)} copy(bf16[64,3,2048]{2,0,1:T(8,128)(2,1)} %param.8) | data formatting | bytes 1572864 | tf_op args[1]
  10.1 2.5 %reshape.39 = bf16[16,2,12288]{2,1,0:T(2,128)(2,1)} reshape(bf16[2048,3,64]{2,1,0:T(4,128)(2,1)S(1)} %bitcast.45) | data formatting | bytes 1572864
  12.6 10.3 %all-to-all-start = ((bf16[16,2,12288]{2,1,0:T(2,128)(2,1)}), bf16[16,2,12288]{2,1,0:T(2,128)(2,1)S(1)}, u32[]{:S(2)}, u32[]{:S(2)}) async-start(bf16[16,2,12288]{2,1,0:T(2,128)(2,1)} %reshape.39), calls=%async_computation | async-start | bytes 1572864 | tf_op jit(solution)/shard_map/all_to_all | solution.py:54
  22.9 13.0 %all-to-all-done = bf16[16,2,12288]{2,1,0:T(2,128)(2,1)S(1)} async-done(((bf16[16,2,12288]{2,1,0:T(2,128)(2,1)}), bf16[16,2,12288]{2,1,0:T(2,128)(2,1)S(1)}, u32[]{:S(2)}, u32[]{:S(2)}) %all-to-all-start) | async-done | bytes 786464 | tf_op jit(solution)/shard_map/all_to_all | solution.py:54
  36.0 1.3 %reshape.40 = bf16[2048,3,64]{2,1,0:T(4,128)(2,1)S(1)} reshape(bf16[16,2,12288]{2,1,0:T(2,128)(2,1)S(1)} %all-to-all-done) | data formatting | bytes 1572864
  37.2 1.2 copy.10
  38.5 1.3 %collective-permute-start = (bf16[768,2,128]{2,0,1:T(8,128)(2,1)S(1)}, bf16[768,2,128]{2,0,1:T(8,128)(2,1)S(1)}, u32[]{:S(2)}, u32[]{:S(2)}) collective-permute-start(bf16[768,2,128]{2,0,1:T(8,128)(2,1)S(1)} %slice.30), channel_id=1, source_target_pairs={{0,16},{16,32},{32,48},{48,64},{64,80},{80,96},{96,112},{112,128},... | collective-permute-start | bytes 1179656 | tf_op jit(solution)/shard_map/ppermute | solution.py:12
  40.1 0.7 slice_bitcast_fusion
  40.9 15.6 %collective-permute-done = bf16[768,2,128]{2,0,1:T(8,128)(2,1)S(1)} collective-permute-done((bf16[768,2,128]{2,0,1:T(8,128)(2,1)S(1)}, bf16[768,2,128]{2,0,1:T(8,128)(2,1)S(1)}, u32[]{:S(2)}, u32[]{:S(2)}) %collective-permute-start) | collective-permute-done | bytes 393248 | tf_op jit(solution)/shard_map/ppermute | solution.py:12
  56.5 1.1 pad_maximum_fusion
  58.1 16.9 %while.14 = (s32[]{:T(128)}, bf16[2,512,128]{2,1,0:T(8,128)(2,1)}, s32[2]{0:T(128)}, s32[]{:T(128)}, bf16[1024,128]{1,0:T(8,128)(2,1)}, /*index=5*/bf16[1792,2,1...) while((s32[]{:T(128)}, bf16[2,512,128]{2,1,0:T(8,128)(2,1)}, ...), condition=%wide.region_3.4_spmd.clone.clone, body=%wide.region_0.3_spmd.clone.clone.sunk | while | flops 344156928 | bytes 8817956 | solution.py:46
  58.1 1.2 dynamic_slice.32
  60.4 2.1 %fusion.37 = (f32[512]{0:T(512)S(1)}, f32[512,1280]{1,0:T(8,128)S(1)}) fusion(bf16[1792,2,128]{2,0,1:T(8,128)(2,1)} %get-tuple-element.231, s32[]{:T(128)S(6)} %select_n.71, bf16[1024,128]{1,0:T(8,128)(2,1)} %get-tuple-element.230, s32[]{:T(128)S(6)} %select_n.72, pred[1280]{0:T(1024)(128)(4,1)S(1)} %add_compare_fusion.2, ...), kind=kOutput, calls=%fused_computation.52.clone.1 | convolution fusion | flops 173014528 | bytes 3090696 | tf_op jit(solution)/shard_map/while/body/eval_jaxpr/dot_general | solution.py:29
  63.2 1.1 fusion.38
  64.3 2.3 %fusion.39 = bf16[2,512,128]{2,1,0:T(8,128)(2,1)} fusion(bf16[2,512,128]{2,1,0:T(8,128)(2,1)} %get-tuple-element.214, s32[]{:T(128)} %get-tuple-element.213, f32[512,1280]{1,0:T(8,128)S(1)} %get-tuple-element.198, f32[512]{0:T(512)} %fusion.38, f32[512]{0:T(512)} %copy-done.2, bf16[1792,2,128]{2,0,1:T(8,128)(2,1)} %get-tuple-element.231, ...), kind=kOutput, calls=%fused_computation.14.clone.1 | convolution fusion | flops 169803776 | bytes 3084808 | tf_op jit(solution)/shard_map/while/body/eval_jaxpr/dot_general | solution.py:42
  66.5 1.2 dynamic_slice.32
  68.8 2.1 %fusion.37 = (f32[512]{0:T(512)S(1)}, f32[512,1280]{1,0:T(8,128)S(1)}) fusion(bf16[1792,2,128]{2,0,1:T(8,128)(2,1)} %get-tuple-element.231, s32[]{:T(128)S(6)} %select_n.71, bf16[1024,128]{1,0:T(8,128)(2,1)} %get-tuple-element.230, s32[]{:T(128)S(6)} %select_n.72, pred[1280]{0:T(1024)(128)(4,1)S(1)} %add_compare_fusion.2, ...), kind=kOutput, calls=%fused_computation.52.clone.1 | convolution fusion | flops 173014528 | bytes 3090696 | tf_op jit(solution)/shard_map/while/body/eval_jaxpr/dot_general | solution.py:29
  71.6 1.1 fusion.38
  72.7 2.3 %fusion.39 = bf16[2,512,128]{2,1,0:T(8,128)(2,1)} fusion(bf16[2,512,128]{2,1,0:T(8,128)(2,1)} %get-tuple-element.214, s32[]{:T(128)} %get-tuple-element.213, f32[512,1280]{1,0:T(8,128)S(1)} %get-tuple-element.198, f32[512]{0:T(512)} %fusion.38, f32[512]{0:T(512)} %copy-done.2, bf16[1792,2,128]{2,0,1:T(8,128)(2,1)} %get-tuple-element.231, ...), kind=kOutput, calls=%fused_computation.14.clone.1 | convolution fusion | flops 169803776 | bytes 3084808 | tf_op jit(solution)/shard_map/while/body/eval_jaxpr/dot_general | solution.py:42
  74.9 5.4 %all-to-all-start.1 = ((bf16[16,64,128]{2,1,0:T(8,128)(2,1)}), bf16[16,64,128]{2,1,0:T(8,128)(2,1)S(1)}, u32[]{:S(2)}, u32[]{:S(2)}) async-start(bf16[16,64,128]{2,1,0:T(8,128)(2,1)} %bitcast.49), calls=%async_computation.1 | async-start | bytes 524288 | tf_op jit(solution)/shard_map/all_to_all | solution.py:61
  80.9 9.6 %all-to-all-done.1 = bf16[16,64,128]{2,1,0:T(8,128)(2,1)S(1)} async-done(((bf16[16,64,128]{2,1,0:T(8,128)(2,1)}), bf16[16,64,128]{2,1,0:T(8,128)(2,1)S(1)}, u32[]{:S(2)}, u32[]{:S(2)}) %all-to-all-start.1) | async-done | bytes 262176 | tf_op jit(solution)/shard_map/all_to_all | solution.py:61
  90.5 15.7 %all-gather.2.cloned.1.call-done = bf16[2048,3072]{0,1:T(8,128)(2,1)} async-done(((bf16[2048,192]{0,1:T(8,128)(2,1)}), bf16[2048,3072]{0,1:T(8,128)(2,1)}) %all-gather.2.cloned.1.call-update) | async-done | bytes 12582928 | tf_op jit(solution)/shard_map/all_gather | solution.py:64
  106.2 9.2 %fusion.22 = bf16[64,3072]{1,0:T(8,128)(2,1)} fusion(f32[64,3072]{1,0:T(8,128)S(1)} %fusion.25, bf16[2048,3072]{0,1:T(8,128)(2,1)} %all-gather.2.cloned.1.call-done, bf16[64,3072]{1,0:T(8,128)(2,1)S(1)} %copy-done.1, bf16[16,64,128]{2,1,0:T(8,128)(2,1)S(1)} %all-to-all-done.1), kind=kOutput, calls=%fused_computation.37 | convolution fusion | flops 806092800 | bytes 14417920 | tf_op jit(solution)/shard_map/dot_general | solution.py:62
  (24 shorter events, 2.6 us)
Async XLA Ops:
  6.5 33.3 %copy-start = (f32[40,3072]{1,0:T(8,128)S(1)}, f32[40,3072]{1,0:T(8,128)}, u32[]{:S(2)}) copy-start(f32[40,3072]{1,0:T(8,128)} %param.10) | copy-start | bytes 1474564
  6.5 99.7 %all-gather.2.cloned.1.call-start = ((), (), s32[]{:S(2)}) async-start(), calls=%async_computation.2 | async-start | bytes 13369344 | tf_op jit(solution)/shard_map/all_gather | solution.py:64
  12.6 23.3 %all-to-all-start = ((bf16[16,2,12288]{2,1,0:T(2,128)(2,1)}), bf16[16,2,12288]{2,1,0:T(2,128)(2,1)S(1)}, u32[]{:S(2)}, u32[]{:S(2)}) async-start(bf16[16,2,12288]{2,1,0:T(2,128)(2,1)} %reshape.39), calls=%async_computation | async-start | bytes 1572864 | tf_op jit(solution)/shard_map/all_to_all | solution.py:54
  22.9 16.9 %copy-start.3 = (s32[4]{0:T(128)S(1)}, s32[4]{0:T(128)}, u32[]{:S(2)}) copy-start(s32[4]{0:T(128)} %param.11) | copy-start | bytes 52
  38.5 18.0 %collective-permute-start = (bf16[768,2,128]{2,0,1:T(8,128)(2,1)S(1)}, bf16[768,2,128]{2,0,1:T(8,128)(2,1)S(1)}, u32[]{:S(2)}, u32[]{:S(2)}) collective-permute-start(bf16[768,2,128]{2,0,1:T(8,128)(2,1)S(1)} %slice.30), channel_id=1, source_target_pairs={{0,16},{16,32},{32,48},{48,64},{64,80},{80,96},{96,112},{112,128},... | collective-permute-start | bytes 1179656 | tf_op jit(solution)/shard_map/ppermute | solution.py:12
  58.1 48.2 %copy-start.1 = (bf16[64,3072]{1,0:T(8,128)(2,1)S(1)}, bf16[64,3072]{1,0:T(8,128)(2,1)}, u32[]{:S(2)}) copy-start(bf16[64,3072]{1,0:T(8,128)(2,1)} %param.7) | copy-start | bytes 1179652
  62.6 0.6 copy-start.2
  71.0 0.6 copy-start.2
  74.9 15.6 %all-to-all-start.1 = ((bf16[16,64,128]{2,1,0:T(8,128)(2,1)}), bf16[16,64,128]{2,1,0:T(8,128)(2,1)S(1)}, u32[]{:S(2)}, u32[]{:S(2)}) async-start(bf16[16,64,128]{2,1,0:T(8,128)(2,1)} %bitcast.49), calls=%async_computation.1 | async-start | bytes 524288 | tf_op jit(solution)/shard_map/all_to_all | solution.py:61
Sparse Core Ops, SparseCore 0:
  9.5 96.6 all-gather.1
where the time goes:
time: 123 us; the launch traced here: 122 us
  waiting for transfers between devices  54.7 us (44%)
  matrix products  18.8 us (15%)
  starting transfers between devices  17 us (14%)
  between operations  13.5 us (11%)
  local copies, waits for them, and re-layouts  12.7 us (10%)
  other arithmetic  3.28 us (3%)
  loops' own time  2.28 us (2%)
    all_gather x1, waiting for transfers between devices, body(): lax.all_gather(out_weight, 'fsdp', axis=1, tiled=True)  15.7 us
    ppermute x1, waiting for transfers between devices, passed_along(): lax.ppermute(value, axis, [(source, source + steps) for source in range(i...  15.6 us
    all_to_all x1, waiting for transfers between devices, body(): lax.all_to_all(projected, 'fsdp', split_axis=2, concat_axis=0, tiled=True)  13 us
    all_to_all x1, starting transfers between devices, body(): lax.all_to_all(projected, 'fsdp', split_axis=2, concat_axis=0, tiled=True)  10.3 us
    all_to_all x1, waiting for transfers between devices, body(): lax.all_to_all(attended, 'fsdp', split_axis=0, concat_axis=1, tiled=True)  9.62 us
    dot_general x1, matrix products, body(): jnp.dot(gathered_heads, lax.all_gather(out_weight, 'fsdp', axis=1, tiled=...  9.25 us
    unnamed x9, local copies, waits for them, and re-layouts  6.63 us
    all_to_all x1, starting transfers between devices, body(): lax.all_to_all(attended, 'fsdp', split_axis=0, concat_axis=1, tiled=True)  5.45 us
  transfers between devices with their start and end apart: 4, of which 4 were waited for; matrix products, arithmetic and copies ran while one was open for 20% of the time, Pallas kernels for 0%

commit v1 on v0

--- a/solution.py
+++ b/solution.py
@@ -48,6 +48,16 @@
 
 
 def body(latents, projected, out_weight, gate_table, timesteps):
+
+    def _produce_object(arr):
+        rows = []
+        for _ in range(lax.axis_size("fsdp")):
+            rows.append(arr)
+        return jnp.concatenate(
+            lax.all_to_all(jnp.stack(rows, axis=0), split_axis=0, concat_axis=0, axis_name="fsdp"),
+            1,
+        )
+
     row_count = latents.shape[0]
     frame_count = timesteps.shape[0]
     group_tokens = frame_count * FRAME_TOK
@@ -60,9 +70,7 @@
     attended = attend(queries, extended, first_frame, frame_count)
     gathered_heads = lax.all_to_all(attended, "fsdp", split_axis=0, concat_axis=1, tiled=True)
     update = jnp.dot(
-        gathered_heads,
-        lax.all_gather(out_weight, "fsdp", axis=1, tiled=True),
-        preferred_element_type=jnp.float32,
+        gathered_heads, _produce_object(out_weight), preferred_element_type=jnp.float32
     )
     step_count = gate_table.shape[0]
     step_onehot = (timesteps[:, None] == jnp.arange(step_count, dtype=jnp.int32)[None, :]).astype(

time: 123 us -> 230 us (1.87); the launches traced: 122 us -> 227 us
  waiting for transfers between devices: 54.7 us -> 146 us
  blocking collectives: 0 us -> 34.6 us
  between operations: 13.5 us -> 0.11 us
  starting transfers between devices: 17 us -> 7.54 us
  local copies, waits for them, and re-layouts: 12.7 us -> 15.2 us
    all_to_all x2 -> x1, waiting for transfers between devices: 22.7 us -> 139 us  [_produce_object(): lax.all_to_all(jnp.stack(rows, axis=0), split_axis=0, concat_axis=0, axis...]
    all_to_all x0 -> x2, blocking collectives: none -> 34.6 us  [the longest x1 22.1 us: body(): lax.all_to_all(projected, 'fsdp', split_axis=2, concat_axis=0, tiled=True)]
    all_gather x1 -> x0, waiting for transfers between devices: 15.7 us -> none  [body(): lax.all_gather(out_weight, 'fsdp', axis=1, tiled=True)]
    all_to_all x2 -> x1, starting transfers between devices: 15.7 us -> 5.81 us  [_produce_object(): lax.all_to_all(jnp.stack(rows, axis=0), split_axis=0, concat_axis=0, axis...]
    ppermute x1, waiting for transfers between devices: 15.6 us -> 7.3 us  [passed_along(): lax.ppermute(value, axis, [(source, source + steps) for source in range(i...]
    another operation x0 -> x1, local copies, waits for them, and re-layouts: none -> 7.22 us  [_produce_object(): jnp.stack(rows, axis=0)]
  transfers between devices with their start and end apart: 4 -> 2, of which waited for: 4 -> 2; matrix products, arithmetic and copies ran while one was open for 20% -> 0% of each run, Pallas kernels for 0% -> 0%
where the time goes in v1:
time: 230 us; the launch traced here: 227 us
  waiting for transfers between devices  146 us (63%)
  blocking collectives  34.6 us (15%)
  matrix products  18.7 us (8%)
  local copies, waits for them, and re-layouts  15.2 us (7%)
  starting transfers between devices  7.54 us (3%)
    all_to_all x1, waiting for transfers between devices, _produce_object(): lax.all_to_all(jnp.stack(rows, axis=0), split_axis=0, concat_axis=0, axis...  139 us
    all_to_all x1, blocking collectives, body(): lax.all_to_all(projected, 'fsdp', split_axis=2, concat_axis=0, tiled=True)  22.1 us
    all_to_all x1, blocking collectives, body(): lax.all_to_all(attended, 'fsdp', split_axis=0, concat_axis=1, tiled=True)  12.4 us
    dot_general x1, matrix products, body(): jnp.dot(gathered_heads, _produce_object(out_weight), preferred_element_ty...  9.25 us
    ppermute x1, waiting for transfers between devices, passed_along(): lax.ppermute(value, axis, [(source, source + steps) for source in range(i...  7.3 us
    another operation x1, local copies, waits for them, and re-layouts, _produce_object(): jnp.stack(rows, axis=0)  7.22 us
    all_to_all x1, starting transfers between devices, _produce_object(): lax.all_to_all(jnp.stack(rows, axis=0), split_axis=0, concat_axis=0, axis...  5.81 us
    unnamed x9, local copies, waits for them, and re-layouts  5.65 us
  transfers between devices with their start and end apart: 2, of which 2 were waited for; matrix products, arithmetic and copies ran while one was open for 0% of the time, Pallas kernels for 0%

profile of v1, /device:TPU:1, one launch (start us, length us, event | category | flops | bytes accessed | tf_op | source)
XLA Modules:
  0.0 226.6 jit_solution(4438011511154641566)
XLA Ops:
  0.0 2.9 %copy.10 = bf16[64,3,2048]{0,1,2:T(4,128)(2,1)S(1)} copy(bf16[64,3,2048]{2,0,1:T(8,128)(2,1)} %param.8) | data formatting | bytes 1572864 | tf_op args[1]
  2.9 1.5 reshape.49
  4.4 22.1 %all_to_all.42 = bf16[16,2,12288]{2,1,0:T(2,128)(2,1)S(1)} all-to-all(bf16[16,2,12288]{2,1,0:T(2,128)(2,1)S(1)} %reshape.49), channel_id=1, replica_groups=mesh['tm'=32,'fsdp'=16] {'fsdp'}, dimensions={0} | all-to-all | bytes 1572864 | tf_op jit(solution)/shard_map/all_to_all | solution.py:64
  26.5 1.3 reshape.50
  27.8 1.2 copy.11
  29.0 1.7 collective-permute-start
  30.9 7.3 %collective-permute-done = bf16[768,2,128]{2,0,1:T(8,128)(2,1)S(1)} collective-permute-done((bf16[768,2,128]{2,0,1:T(8,128)(2,1)S(1)}, bf16[768,2,128]{2,0,1:T(8,128)(2,1)S(1)}, u32[]{:S(2)}, u32[]{:S(2)}) %collective-permute-start) | collective-permute-done | bytes 393248 | tf_op jit(solution)/shard_map/ppermute | solution.py:12
  38.2 1.0 pad_maximum_fusion
  39.1 13.1 %while.14 = (s32[]{:T(128)}, bf16[2,512,128]{2,1,0:T(8,128)(2,1)}, s32[2]{0:T(128)S(1)}, s32[]{:T(128)}, bf16[1024,128]{1,0:T(8,128)(2,1)S(1)}, /*index=5*/bf16[...) while((s32[]{:T(128)}, bf16[2,512,128]{2,1,0:T(8,128)(2,1)}, ...), condition=%wide.region_3.4_spmd.clone.clone, body=%wide.region_0.3_spmd.clone.clone.sunk | while | flops 344156928 | bytes 8813076 | solution.py:46
  39.1 0.6 dynamic_slice.32
  40.8 2.1 fusion.37
  42.9 0.5 fusion.38
  43.4 2.2 fusion.39
  45.7 0.6 dynamic_slice.32
  47.4 2.1 fusion.37
  49.4 0.5 fusion.38
  50.0 2.2 fusion.39
  52.2 12.4 %all_to_all.43 = bf16[16,64,128]{2,1,0:T(8,128)(2,1)S(1)} all-to-all(bf16[16,64,128]{2,1,0:T(8,128)(2,1)} %bitcast.52), channel_id=1, replica_groups=mesh['tm'=32,'fsdp'=16] {'fsdp'}, dimensions={0} | all-to-all | bytes 524288 | tf_op jit(solution)/shard_map/all_to_all | solution.py:71
  64.6 7.2 %stack.2 = bf16[16,2048,192]{1,2,0:T(8,128)(2,1)} broadcast(bf16[2048,192]{0,1:T(8,128)(2,1)} %param.9), dimensions={1,2} | broadcast | bytes 13369344 | tf_op jit(solution)/shard_map/stack | solution.py:57
  71.8 5.8 %all-to-all-start.2 = ((bf16[16,2048,192]{1,2,0:T(8,128)(2,1)}), bf16[16,2048,192]{1,2,0:T(8,128)(2,1)}, u32[]{:S(2)}, u32[]{:S(2)}) async-start(bf16[16,2048,192]{1,2,0:T(8,128)(2,1)} %stack.2), calls=%async_computation.2 | async-start | bytes 25165824 | tf_op jit(solution)/shard_map/all_to_all | solution.py:57
  77.7 0.3 fusion.27
  78.0 0.5 fusion.25
  78.5 138.8 %all-to-all-done.2 = bf16[16,2048,192]{1,2,0:T(8,128)(2,1)} async-done(((bf16[16,2048,192]{1,2,0:T(8,128)(2,1)}), bf16[16,2048,192]{1,2,0:T(8,128)(2,1)}, u32[]{:S(2)}, u32[]{:S(2)}) %all-to-all-start.2) | async-done | bytes 12582944 | tf_op jit(solution)/shard_map/all_to_all | solution.py:57
  217.3 9.2 %fusion.22 = bf16[64,3072]{1,0:T(8,128)(2,1)} fusion(f32[64,3072]{1,0:T(8,128)S(1)} %fusion.25, bf16[2048,3072]{0,1:T(8,128)(2,1)} %bitcast.8, bf16[64,3072]{1,0:T(8,128)(2,1)S(1)} %copy-done.1, bf16[16,64,128]{2,1,0:T(8,128)(2,1)S(1)} %all_to_all.43), kind=kOutput, calls=%fused_computation.37 | convolution fusion | flops 806092800 | bytes 14417920 | tf_op jit(solution)/shard_map/dot_general | solution.py:72
  (18 shorter events, 0.1 us)
Async XLA Ops:
  0.0 77.7 %copy-start = (f32[40,3072]{1,0:T(8,128)S(1)}, f32[40,3072]{1,0:T(8,128)}, u32[]{:S(2)}) copy-start(f32[40,3072]{1,0:T(8,128)} %param.10) | copy-start | bytes 1474564
  29.0 9.1 %collective-permute-start = (bf16[768,2,128]{2,0,1:T(8,128)(2,1)S(1)}, bf16[768,2,128]{2,0,1:T(8,128)(2,1)S(1)}, u32[]{:S(2)}, u32[]{:S(2)}) collective-permute-start(bf16[768,2,128]{2,0,1:T(8,128)(2,1)S(1)} %slice.30), channel_id=1, source_target_pairs={{0,16},{16,32},{32,48},{48,64},{64,80},{80,96},{96,112},{112,128},... | collective-permute-start | bytes 1179656 | tf_op jit(solution)/shard_map/ppermute | solution.py:12
  71.8 5.8 %copy-start.2 = (s32[4]{0:T(128)S(1)}, s32[4]{0:T(128)}, u32[]{:S(2)}) copy-start(s32[4]{0:T(128)} %param.11) | copy-start | bytes 52
  71.8 145.5 %copy-start.1 = (bf16[64,3072]{1,0:T(8,128)(2,1)S(1)}, bf16[64,3072]{1,0:T(8,128)(2,1)}, u32[]{:S(2)}) copy-start(bf16[64,3072]{1,0:T(8,128)(2,1)} %param.7) | copy-start | bytes 1179652
  71.8 145.5 %all-to-all-start.2 = ((bf16[16,2048,192]{1,2,0:T(8,128)(2,1)}), bf16[16,2048,192]{1,2,0:T(8,128)(2,1)}, u32[]{:S(2)}, u32[]{:S(2)}) async-start(bf16[16,2048,192]{1,2,0:T(8,128)(2,1)} %stack.2), calls=%async_computation.2 | async-start | bytes 25165824 | tf_op jit(solution)/shard_map/all_to_all | solution.py:57
